TPU v7x, 256 devices: a whole 4x4x8 slice. The times are simulated.
256 devices in a mesh: row: 32 (over z, y), col: 8 (over x, core).
Axes of the slice: x: 4, y: 4, z: 8, core: 2. Of those that a mesh axis runs over, the one named last changes fastest.
Arguments:
- saved_input: bfloat16 [1024, 49152], P('col', 'row'), may hold values from -6 to 6
- out_grad: bfloat16 [1024, 12288], P('row', 'col'), may hold values from -0.75 to 0.75
- weight: bfloat16 [49152, 12288], P('row', 'col'), may hold values from -0.625 to 0.625
Outputs:
- in_grad: bfloat16 [1024, 49152], P('col', 'row')
- weight_grad: bfloat16 [49152, 12288], P('row', 'col')
All inputs are finite; a program needn't handle non-finite values.
Results may differ from a plain program's by a relative error of at most 0.0051.
Values may be sent and summed in bfloat16 or wider, within the bound.
No kernel may reach another device: no remote copies, remote signals or barrier semaphores. Data moves between devices by JAX's collectives and lax.ppermute only.
A program may use at most 64 MiB of HBM per device.

v0:
```python
import math
import jax
import jax.numpy as jnp
from jax import lax
from jax.sharding import PartitionSpec as P


def gelu_parts(values):
    coeff = math.sqrt(2.0 / math.pi)
    inner = jnp.tanh(coeff * (values + 0.044715 * values * values * values))
    gelu_value = 0.5 * values * (1.0 + inner)
    gelu_slope = 0.5 * (1.0 + inner) + 0.5 * values * (1.0 - inner * inner) * coeff * (
        1.0 + 3.0 * 0.044715 * values * values
    )
    return (gelu_value, gelu_slope)


def per_device(saved_input, out_grad, weight):
    grad_all = lax.all_gather(out_grad, "row", axis=0, tiled=True)
    saved_all = lax.all_gather(saved_input, "col", axis=0, tiled=True)
    gelu_value, unused_slope = gelu_parts(saved_all.astype(jnp.float32))
    hidden = gelu_value.astype(jnp.bfloat16)
    weight_grad = lax.dot_general(
        hidden, grad_all, (((0,), (0,)), ((), ())), preferred_element_type=jnp.float32
    ).astype(jnp.bfloat16)
    back = lax.psum_scatter(
        lax.dot_general(
            grad_all, weight, (((1,), (1,)), ((), ())), preferred_element_type=jnp.float32
        ),
        "col",
        scatter_dimension=0,
        tiled=True,
    )
    unused_value, own_slope = gelu_parts(saved_input.astype(jnp.float32))
    in_grad = (back * own_slope).astype(jnp.bfloat16)
    return (in_grad, weight_grad)


def solution(mesh):
    in_specs = (P("col", "row"), P("row", "col"), P("row", "col"))
    out_specs = (P("col", "row"), P("row", "col"))
    return jax.shard_map(
        per_device, mesh=mesh, in_specs=in_specs, out_specs=out_specs, check_vma=False
    )
```

profile of v0, /device:TPU:1, one launch (start us, length us, event | category | flops | bytes accessed | tf_op | source)
XLA Modules:
  0.0 178.5 jit_solution(13680003618552402031)
XLA Ops:
  7.2 0.0 all-gather.3.cloned.1.call-start
  7.2 0.7 all-gather.3.cloned.1.call-update
  7.9 0.0 all-gather.5.cloned.1.call-start
  7.9 0.7 all-gather.5.cloned.1.call-update
  8.6 0.0 reduce-scatter.2.cloned.1.call-start
  8.7 81.3 %all-gather.3.cloned.1.call-done = bf16[1024,1536]{1,0:T(8,128)(2,1)} async-done(((bf16[32,1536]{1,0:T(8,128)(2,1)}), bf16[1024,1536]{1,0:T(8,128)(2,1)}) %all-gather.3.cloned.1.call-update) | async-done | bytes 3145744 | tf_op jit(solution)/shard_map/all_gather | solution.py:19
  90.0 9.8 %fusion.23 = f32[1024,1536]{1,0:T(8,128)} fusion(bf16[1024,1536]{1,0:T(8,128)(2,1)} %all-gather.3.cloned.1.call-done, bf16[1536,1536]{1,0:T(8,128)(2,1)} %param.5), kind=kOutput, calls=%fused_computation.35 | convolution fusion | flops 4831838208 | bytes 14155776 | tf_op jit(solution)/shard_map/dot_general | solution.py:27
  99.7 0.0 copy-start.1
  99.7 0.0 reduce-scatter.2.cloned.1.call-update
  99.8 0.0 copy-start
  99.8 23.2 %all-gather.5.cloned.1.call-done = bf16[1024,1536]{1,0:T(8,128)(2,1)} async-done(((bf16[128,1536]{1,0:T(8,128)(2,1)}), bf16[1024,1536]{1,0:T(8,128)(2,1)}) %all-gather.5.cloned.1.call-update) | async-done | bytes 3145744 | tf_op jit(solution)/shard_map/all_gather | solution.py:20
  122.9 0.0 copy-done.1
  122.9 11.2 %convolution_convert_fusion = bf16[1536,1536]{1,0:T(8,128)(2,1)} fusion(bf16[1024,1536]{1,0:T(8,128)(2,1)S(1)} %copy-done.1, bf16[1024,1536]{1,0:T(8,128)(2,1)} %all-gather.5.cloned.1.call-done), kind=kOutput, calls=%fused_computation.5 | convolution fusion | flops 4849926144 | bytes 11010048 | tf_op jit(solution)/shard_map/dot_general | solution.py:23
  134.2 35.4 %reduce-scatter.2.cloned.1.call-done = f32[128,1536]{1,0:T(8,128)} async-done(((f32[1024,1536]{1,0:T(8,128)}), f32[128,1536]{1,0:T(8,128)}) %reduce-scatter.2.cloned.1.call-update) | async-done | bytes 786448 | tf_op jit(solution)/shard_map/reduce_scatter | solution.py:26
  169.6 0.0 copy-done
  169.6 2.4 %fusion.17 = bf16[128,1536]{1,0:T(8,128)(2,1)} fusion(f32[128,1536]{1,0:T(8,128)} %reduce-scatter.2.cloned.1.call-done, bf16[128,1536]{1,0:T(8,128)(2,1)S(1)} %copy-done), kind=kLoop, calls=%fused_computation.29 | loop fusion | flops 3932160 | bytes 1572864 | tf_op jit(solution)/shard_map/convert_element_type | solution.py:35
Async XLA Ops:
  7.2 82.8 %all-gather.3.cloned.1.call-start = ((), (), s32[]{:S(2)}) async-start(), calls=%async_computation.1 | async-start | bytes 3244032 | tf_op jit(solution)/shard_map/all_gather | solution.py:19
  7.9 115.0 %all-gather.5.cloned.1.call-start = ((), (), s32[]{:S(2)}) async-start(), calls=%async_computation.3 | async-start | bytes 3538944 | tf_op jit(solution)/shard_map/all_gather | solution.py:20
  8.6 161.0 %reduce-scatter.2.cloned.1.call-start = ((), (), s32[]{:S(2)}) async-start(), calls=%async_computation.2 | async-start | bytes 7077888 | tf_op jit(solution)/shard_map/reduce_scatter | solution.py:26
  99.7 23.2 %copy-start.1 = (bf16[1024,1536]{1,0:T(8,128)(2,1)S(1)}, bf16[1024,1536]{1,0:T(8,128)(2,1)}, u32[]{:S(2)}) copy-start(bf16[1024,1536]{1,0:T(8,128)(2,1)} %all-gather.3.cloned.1.call-done) | copy-start | bytes 9437188
  99.8 69.8 %copy-start = (bf16[128,1536]{1,0:T(8,128)(2,1)S(1)}, bf16[128,1536]{1,0:T(8,128)(2,1)}, u32[]{:S(2)}) copy-start(bf16[128,1536]{1,0:T(8,128)(2,1)} %param.3) | copy-start | bytes 1179652
Sparse Core Ops, SparseCore 0:
  10.5 79.3 all-gather.2
  91.8 31.1 all-gather.4
  125.5 44.0 reduce-scatter.1
where the time goes:
time: 179 us
  waiting for transfers between devices  141 us (79%)
  matrix products  21 us (12%)
  between operations  13.8 us (8%)
  other arithmetic  2.4 us (1%)
    all_gather x1, waiting for transfers between devices, per_device(): grad_all = lax.all_gather(out_grad, 'row', axis=0, tiled=True)  81.3 us
    reduce_scatter x1, waiting for transfers between devices, per_device(): lax.psum_scatter(lax.dot_general(grad_all, weight, (((1,), (1,)), ((), ()...  35.4 us
    all_gather x1, waiting for transfers between devices, per_device(): saved_all = lax.all_gather(saved_input, 'col', axis=0, tiled=True)  23.2 us
    dot_general x1, matrix products, per_device(): lax.dot_general(hidden, grad_all, (((0,), (0,)), ((), ())), preferred_ele...  11.2 us
    dot_general x1, matrix products, per_device(): lax.dot_general(grad_all, weight, (((1,), (1,)), ((), ())), preferred_ele...  9.78 us
  transfers between devices with their start and end apart: 3, of which 3 were waited for; matrix products, arithmetic and copies ran while one was open for 12% of the time, Pallas kernels for 0%

commit v1 on v0

--- a/solution.py
+++ b/solution.py
@@ -17,7 +17,12 @@
 
 def per_device(saved_input, out_grad, weight):
     grad_all = lax.all_gather(out_grad, "row", axis=0, tiled=True)
-    saved_all = lax.all_gather(saved_input, "col", axis=0, tiled=True)
+    saved_all = jnp.concatenate(
+        lax.all_to_all(
+            jnp.stack([saved_input] * lax.axis_size("col"), 0), "col", concat_axis=0, split_axis=0
+        ),
+        0,
+    )
     gelu_value, unused_slope = gelu_parts(saved_all.astype(jnp.float32))
     hidden = gelu_value.astype(jnp.bfloat16)
     weight_grad = lax.dot_general(

time: 179 us -> 186 us (1.039)
  blocking collectives: 0 us -> 62.3 us
  waiting for transfers between devices: 141 us -> 89.1 us
  matrix products: 21 us -> 17.1 us
    all_to_all x0 -> x1, blocking collectives: none -> 62.3 us  [per_device(): lax.all_to_all(jnp.stack([saved_input] * lax.axis_size('col'), 0), 'col',...]
    reduce_scatter x1, waiting for transfers between devices: 35.4 us -> 6.37 us  [per_device(): lax.psum_scatter(lax.dot_general(grad_all, weight, (((1,), (1,)), ((), ()...]
    all_gather x1 -> x0, waiting for transfers between devices: 23.2 us -> none  [per_device(): saved_all = lax.all_gather(saved_input, 'col', axis=0, tiled=True)]
    dot_general x1, matrix products: 11.2 us -> 7.33 us  [per_device(): lax.dot_general(hidden, grad_all, (((0,), (0,)), ((), ())), preferred_ele...]
  transfers between devices with their start and end apart: 3 -> 2, of which waited for: 3 -> 2; matrix products, arithmetic and copies ran while one was open for 12% -> 4% of each run, Pallas kernels for 0% -> 0%
where the time goes in v1:
time: 186 us
  waiting for transfers between devices  89.1 us (48%)
  blocking collectives  62.3 us (33%)
  matrix products  17.1 us (9%)
  between operations  14 us (8%)
  other arithmetic  2.4 us (1%)
    all_gather x1, waiting for transfers between devices, per_device(): grad_all = lax.all_gather(out_grad, 'row', axis=0, tiled=True)  82 us
    all_to_all x1, blocking collectives, per_device(): lax.all_to_all(jnp.stack([saved_input] * lax.axis_size('col'), 0), 'col',...  62.3 us
    dot_general x1, matrix products, per_device(): lax.dot_general(grad_all, weight, (((1,), (1,)), ((), ())), preferred_ele...  9.76 us
    dot_general x1, matrix products, per_device(): lax.dot_general(hidden, grad_all, (((0,), (0,)), ((), ())), preferred_ele...  7.33 us
    reduce_scatter x1, waiting for transfers between devices, per_device(): lax.psum_scatter(lax.dot_general(grad_all, weight, (((1,), (1,)), ((), ()...  6.37 us
  transfers between devices with their start and end apart: 2, of which 2 were waited for; matrix products, arithmetic and copies ran while one was open for 4% of the time, Pallas kernels for 0%

profile of v1, /device:TPU:1, one launch (start us, length us, event | category | flops | bytes accessed | tf_op | source)
XLA Modules:
  0.0 186.3 jit_solution(5535786687496310755)
XLA Ops:
  7.2 0.0 all-gather.2.cloned.1.call-start
  7.2 0.7 all-gather.2.cloned.1.call-update
  7.9 0.0 reduce-scatter.2.cloned.1.call-start
  7.9 82.0 %all-gather.2.cloned.1.call-done = bf16[1024,1536]{1,0:T(8,128)(2,1)} async-done(((bf16[32,1536]{1,0:T(8,128)(2,1)}), bf16[1024,1536]{1,0:T(8,128)(2,1)}) %all-gather.2.cloned.1.call-update) | async-done | bytes 3145744 | tf_op jit(solution)/shard_map/all_gather | solution.py:19
  90.0 9.8 %fusion.23 = f32[1024,1536]{1,0:T(8,128)} fusion(bf16[1024,1536]{1,0:T(8,128)(2,1)} %all-gather.2.cloned.1.call-done, bf16[1536,1536]{1,0:T(8,128)(2,1)} %param.5), kind=kOutput, calls=%fused_computation.35 | convolution fusion | flops 4831838208 | bytes 14155776 | tf_op jit(solution)/shard_map/dot_general | solution.py:32
  99.7 0.0 copy-start
  99.7 0.0 reduce-scatter.2.cloned.1.call-update
  99.7 1.0 copy-done
  100.7 0.0 copy-start.1
  100.7 0.3 stack.2
  101.0 62.3 %all_to_all.5 = bf16[8,128,1536]{2,1,0:T(8,128)(2,1)S(1)} all-to-all(bf16[8,128,1536]{2,1,0:T(8,128)(2,1)S(1)} %stack.2), channel_id=1, replica_groups=mesh['row'=32,'col'=8] {'col'}, dimensions={0} | all-to-all | bytes 6291456 | tf_op jit(solution)/shard_map/all_to_all | solution.py:21
  163.3 0.0 copy-done.1
  163.3 7.3 %convolution_convert_fusion = bf16[1536,1536]{1,0:T(8,128)(2,1)} fusion(bf16[1024,1536]{1,0:T(8,128)(2,1)S(1)} %copy-done.1, bf16[1024,1536]{1,0:T(8,128)(2,1)S(1)} %bitcast.5), kind=kOutput, calls=%fused_computation.5 | convolution fusion | flops 4849926144 | bytes 11010048 | tf_op jit(solution)/shard_map/dot_general | solution.py:28
  170.6 6.4 %reduce-scatter.2.cloned.1.call-done = f32[128,1536]{1,0:T(8,128)} async-done(((f32[1024,1536]{1,0:T(8,128)}), f32[128,1536]{1,0:T(8,128)}) %reduce-scatter.2.cloned.1.call-update) | async-done | bytes 786448 | tf_op jit(solution)/shard_map/reduce_scatter | solution.py:31
  177.0 2.4 %fusion.17 = bf16[128,1536]{1,0:T(8,128)(2,1)} fusion(f32[128,1536]{1,0:T(8,128)} %reduce-scatter.2.cloned.1.call-done, bf16[128,1536]{1,0:T(8,128)(2,1)S(1)} %copy-done), kind=kLoop, calls=%fused_computation.29 | loop fusion | flops 3932160 | bytes 1572864 | tf_op jit(solution)/shard_map/convert_element_type | solution.py:40
Async XLA Ops:
  7.2 82.8 %all-gather.2.cloned.1.call-start = ((), (), s32[]{:S(2)}) async-start(), calls=%async_computation.2 | async-start | bytes 3244032 | tf_op jit(solution)/shard_map/all_gather | solution.py:19
  7.9 169.1 %reduce-scatter.2.cloned.1.call-start = ((), (), s32[]{:S(2)}) async-start(), calls=%async_computation.3 | async-start | bytes 7077888 | tf_op jit(solution)/shard_map/reduce_scatter | solution.py:31
  99.7 1.0 copy-start
  100.7 62.6 %copy-start.1 = (bf16[1024,1536]{1,0:T(8,128)(2,1)S(1)}, bf16[1024,1536]{1,0:T(8,128)(2,1)}, u32[]{:S(2)}) copy-start(bf16[1024,1536]{1,0:T(8,128)(2,1)} %all-gather.2.cloned.1.call-done) | copy-start | bytes 9437188
Sparse Core Ops, SparseCore 0:
  10.5 79.3 all-gather.1
  99.9 77.1 reduce-scatter.1
